TPU v7x, 512 devices: a whole 4x4x16 slice. The times are simulated.
512 devices in a mesh: expert: 8 (over y, core), mp: 64 (over x, z).
Axes of the slice: x: 4, y: 4, z: 16, core: 2. Of those that a mesh axis runs over, the one named last changes fastest.
Arguments:
- context: bfloat16 [4096, 2048], P('expert', 'mp'), may hold values from -6 to 6
- out_proj: bfloat16 [2048, 2048], P('mp'), may hold values from -1 to 1, as said below
- routes: int32 [4096, 2], P('expert'), may hold values from 0 to 7, all different within a row; in each aligned block of 512 rows (0 to 511, 512 to 1023, ...) at most 256 rows name the same one
- router_logits: float32 [4096, 2], P('expert'), may hold values from -8 to 8
- w_gate: bfloat16 [45056, 2048], P('mp', 'expert'), may hold values from -0.125 to 0.125
- w_up: bfloat16 [45056, 2048], P('mp', 'expert'), may hold values from -0.125 to 0.125
- w_down: bfloat16 [45056, 2048], P('mp', 'expert'), may hold values from -0.078125 to 0.078125
- norm_gain: float32 [2048], P('mp'), may hold values from 0.25 to 1.75
- request_order: int32 [4096], P('expert'), may hold values from 0 to 4095, each once
Outputs:
- restored: bfloat16 [4096, 2048], P('expert', 'mp')
Inputs may be any that keep to these rules, and one draw needn't show every extreme that they name: `routes`: each row names 2 different experts. Within each aligned block of 512 rows no expert is named by more than 256 rows, and in some blocks one expert is named by exactly 256 rows. `request_order`: A permutation of the 4096 token rows. `out_proj`: entries of the order of one over the square root of 2048.
All inputs are finite; a program needn't handle non-finite values.
Results may differ from a plain program's by a relative error of at most 0.0056.
Values may be sent and summed in bfloat16 or wider, within the bound.
No kernel may reach another device: no remote copies, remote signals or barrier semaphores. Data moves between devices by JAX's collectives and lax.ppermute only.
A program may use at most 64 MiB of HBM per device.

v0:
```python
import jax
import jax.numpy as jnp
from jax import lax
from jax.sharding import PartitionSpec as P

EXPERTS = 8
CAP = 256
epsilon = 1e-06


def slot_targets(routes, capacity, experts):
    flat_routes = routes.reshape(-1)
    onehot = (flat_routes[:, None] == jnp.arange(experts, dtype=jnp.int32)[None, :]).astype(
        jnp.int32
    )
    earlier = jnp.cumsum(onehot, axis=0) - onehot
    slot_index = jnp.sum(earlier * onehot, axis=1)
    return flat_routes * capacity + slot_index


def shards(
    context, out_proj, routes, router_logits, w_gate, w_up, w_down, norm_gain, request_order
):
    tok_rows = context.shape[0]
    feat_local = context.shape[1]
    model_width = out_proj.shape[1]
    mp_count = lax.axis_size("mp")
    copies = mp_count // EXPERTS
    capacity = CAP
    top_k = routes.shape[1]
    attended = jnp.einsum(
        "td,cd->tc",
        lax.all_gather(context, "mp", axis=1, tiled=True),
        out_proj,
        preferred_element_type=jnp.float32,
    ).astype(jnp.bfloat16)
    destination = slot_targets(routes, capacity, EXPERTS)
    source_rows = jnp.repeat(jnp.arange(tok_rows, dtype=jnp.int32), top_k)
    slotted = (
        jnp.zeros((EXPERTS * capacity, feat_local), jnp.bfloat16)
        .at[destination]
        .set(attended[source_rows])
    )
    slotted = jnp.repeat(slotted.reshape(EXPERTS, capacity, feat_local), copies, axis=0)
    outgoing = slotted.transpose(1, 0, 2).reshape(capacity, mp_count * feat_local)
    inbox_rows = lax.all_to_all(outgoing, "mp", split_axis=1, concat_axis=1, tiled=True)
    gate_next = jnp.einsum(
        "rd,hd->rh",
        inbox_rows,
        lax.all_gather(w_gate, "expert", axis=1, tiled=True),
        preferred_element_type=jnp.float32,
    )
    up_next = jnp.einsum(
        "rd,hd->rh",
        inbox_rows,
        lax.all_gather(w_up, "expert", axis=1, tiled=True),
        preferred_element_type=jnp.float32,
    )
    activated = (jax.nn.silu(gate_next) * up_next).astype(jnp.bfloat16)
    partial_value = jnp.dot(
        activated,
        lax.all_gather(w_down, "expert", axis=1, tiled=True),
        preferred_element_type=jnp.float32,
    )
    returned = lax.all_to_all(partial_value, "mp", split_axis=1, concat_axis=0, tiled=True)
    expert_out = jnp.sum(returned.reshape(EXPERTS, copies, capacity, feat_local), axis=1).reshape(
        EXPERTS * capacity, feat_local
    )
    picked = expert_out[destination].reshape(tok_rows, top_k, feat_local)
    weights = 1.0 / (1.0 + jnp.exp(router_logits[:, ::-1] - router_logits))
    branch = jnp.sum(picked * weights[:, :, None], axis=1)
    combined = attended.astype(jnp.float32) + branch
    squares = lax.psum(jnp.sum(combined * combined, axis=1), "mp")
    normed = (
        combined * norm_gain[None, :] * lax.rsqrt(squares / model_width + epsilon)[:, None]
    ).astype(jnp.bfloat16)
    everyone = lax.all_gather(normed, "expert", axis=0, tiled=True)
    return everyone[request_order]


def solution(mesh):
    placed = (
        P("expert", "mp"),
        P("mp", None),
        P("expert", None),
        P("expert", None),
        P("mp", "expert"),
        P("mp", "expert"),
        P("mp", "expert"),
        P("mp"),
        P("expert"),
    )
    return jax.shard_map(
        shards, mesh=mesh, in_specs=placed, out_specs=P("expert", "mp"), check_vma=False
    )
```

profile of v0, /device:TPU:1, one launch (start us, length us, event | category | flops | bytes accessed | tf_op | source)
XLA Modules:
  0.0 565.7 jit_solution(14208333560372502879)
XLA Ops:
  6.5 0.7 all-gather.5.cloned.1.call-update
  7.3 0.7 all-gather.7.cloned.1.call-update
  8.1 0.7 all-gather.11.cloned.1.call-update
  8.8 0.5 all-gather.9.cloned.1.call-update
  9.3 0.8 copy.42
  10.5 0.7 broadcast_multiply_fusion
  11.2 2.3 reduce-window.6
  13.5 0.3 slice_reduce_fusion
  14.1 0.2 mul.55
  14.4 0.2 reshape.104
  14.6 133.1 %all-gather.5.cloned.1.call-done = bf16[512,2048]{0,1:T(8,128)(2,1)} async-done(((bf16[512,32]{0,1:T(8,128)(2,1)}), bf16[512,2048]{0,1:T(8,128)(2,1)}) %all-gather.5.cloned.1.call-update) | async-done | bytes 2097168 | tf_op jit(solution)/shard_map/all_gather | solution.py:33
  147.7 2.0 convolution_convert_fusion
  149.9 6.4 %scatter_custom_fusion = bf16[2048,32]{1,0:T(8,128)(2,1)S(1)} fusion(s32[1024]{0:T(1024)S(1)} %bitcast.48, bf16[512,32]{1,0:T(8,128)(2,1)S(1)} %copy.44, s32[1024]{0:T(1024)S(1)} %broadcast_clamp_fusion.1, bf16[]{:T(256)} %constant.10.clone.1), kind=kCustom, calls=%fused_computation.16 | custom fusion | bytes 131074 | tf_op jit(solution)/shard_map/scatter | solution.py:42
  156.3 0.2 copy.46
  156.5 1.2 broadcast_in_dim.10
  157.7 8.8 %all-to-all-start = ((bf16[256,64,32]{0,2,1:T(8,128)(2,1)}), bf16[256,64,32]{0,2,1:T(8,128)(2,1)S(1)}, u32[]{:S(2)}, u32[]{:S(2)}) async-start(bf16[256,64,32]{0,2,1:T(8,128)(2,1)} %bitcast.6), calls=%async_computation | async-start | bytes 2097152 | tf_op jit(solution)/shard_map/all_to_all | solution.py:46
  166.5 26.9 %all-gather.7.cloned.1.call-done = bf16[704,2048]{1,0:T(8,128)(2,1)} async-done(((bf16[704,256]{1,0:T(8,128)(2,1)}), bf16[704,2048]{1,0:T(8,128)(2,1)}) %all-gather.7.cloned.1.call-update) | async-done | bytes 2883600 | tf_op jit(solution)/shard_map/all_gather | solution.py:50
  193.4 12.3 %all-to-all-done = bf16[256,64,32]{0,2,1:T(8,128)(2,1)S(1)} async-done(((bf16[256,64,32]{0,2,1:T(8,128)(2,1)}), bf16[256,64,32]{0,2,1:T(8,128)(2,1)S(1)}, u32[]{:S(2)}, u32[]{:S(2)}) %all-to-all-start) | async-done | bytes 1048608 | tf_op jit(solution)/shard_map/all_to_all | solution.py:46
  205.6 2.7 fusion.16
  208.4 26.4 %all-gather.11.cloned.1.call-done = bf16[704,2048]{1,0:T(8,128)(2,1)} async-done(((bf16[704,256]{1,0:T(8,128)(2,1)}), bf16[704,2048]{1,0:T(8,128)(2,1)}) %all-gather.11.cloned.1.call-update) | async-done | bytes 2883600 | tf_op jit(solution)/shard_map/all_gather | solution.py:62
  234.8 41.3 %all-gather.9.cloned.1.call-done = bf16[704,2048]{1,0:T(8,128)(2,1)} async-done(((bf16[704,256]{1,0:T(8,128)(2,1)}), bf16[704,2048]{1,0:T(8,128)(2,1)}) %all-gather.9.cloned.1.call-update) | async-done | bytes 2883600 | tf_op jit(solution)/shard_map/all_gather | solution.py:56
  276.1 7.2 %fusion.1 = f32[256,2048]{0,1:T(8,128)} fusion(bf16[704,2048]{1,0:T(8,128)(2,1)} %all-gather.11.cloned.1.call-done, bf16[704,2048]{1,0:T(8,128)(2,1)} %all-gather.9.cloned.1.call-done, bf16[256,2048]{0,1:T(8,128)(2,1)S(1)} %bitcast.46, f32[256,704]{0,1:T(8,128)S(1)} %fusion.16), kind=kOutput, calls=%fused_computation.8 | convolution fusion | flops 1477476352 | bytes 9633792 | tf_op jit(solution)/shard_map/dot_general | solution.py:60
  283.4 15.6 %all-to-all-start.1 = ((f32[256,64,32]{0,2,1:T(8,128)}), f32[256,64,32]{0,2,1:T(8,128)S(1)}, u32[]{:S(2)}, u32[]{:S(2)}) async-start(f32[256,64,32]{0,2,1:T(8,128)} %bitcast.43), calls=%async_computation.1 | async-start | bytes 4194304 | tf_op jit(solution)/shard_map/all_to_all | solution.py:65
  299.4 91.4 %all-to-all-done.1 = f32[256,64,32]{0,2,1:T(8,128)S(1)} async-done(((f32[256,64,32]{0,2,1:T(8,128)}), f32[256,64,32]{0,2,1:T(8,128)S(1)}, u32[]{:S(2)}, u32[]{:S(2)}) %all-to-all-start.1) | async-done | bytes 2097184 | tf_op jit(solution)/shard_map/all_to_all | solution.py:65
  390.9 0.3 copy.48
  391.3 2.8 gather_fusion
  394.1 2.8 multiply_reduce_fusion
  397.1 118.5 %psum.7 = f32[512]{0:T(512)S(1)} all-reduce(f32[512]{0:T(512)S(1)} %multiply_reduce_fusion.1), channel_id=1, replica_groups=mesh['expert'=8,'mp'=64] {'mp'}, use_global_device_ids=true, to_apply=%region_7.8 | all-reduce | flops 512 | bytes 4096 | tf_op jit(solution)/shard_map/psum | solution.py:73
  515.6 41.0 %all_gather.19 = bf16[4096,32]{0,1:T(8,128)(2,1)S(1)} all-gather(bf16[512,32]{0,1:T(8,128)(2,1)S(1)} %multiply_convert_fusion), channel_id=1, replica_groups=mesh['expert'=8,'mp'=64] {'expert'}, dimensions={0}, use_global_device_ids=true | all-gather | bytes 294912 | tf_op jit(solution)/shard_map/all_gather | solution.py:77
  556.6 0.5 copy.51
  557.1 1.3 gather_fusion.1
  558.4 0.7 copy.52
  (35 shorter events, 1.8 us)
Async XLA Ops:
  6.5 141.2 %copy-start = (bf16[32,2048]{1,0:T(8,128)(2,1)S(1)}, bf16[32,2048]{1,0:T(8,128)(2,1)}, u32[]{:S(2)}) copy-start(bf16[32,2048]{1,0:T(8,128)(2,1)} %param.10) | copy-start | bytes 393220
  6.5 141.2 %all-gather.5.cloned.1.call-start = ((), (), s32[]{:S(2)}) async-start(), calls=%async_computation.2 | async-start | bytes 2129920 | tf_op jit(solution)/shard_map/all_gather | solution.py:33
  7.3 186.1 %all-gather.7.cloned.1.call-start = ((), (), s32[]{:S(2)}) async-start(), calls=%async_computation.3 | async-start | bytes 3244032 | tf_op jit(solution)/shard_map/all_gather | solution.py:50
  8.0 226.8 %all-gather.11.cloned.1.call-start = ((), (), s32[]{:S(2)}) async-start(), calls=%async_computation.5 | async-start | bytes 3244032 | tf_op jit(solution)/shard_map/all_gather | solution.py:62
  8.7 267.4 %all-gather.9.cloned.1.call-start = ((), (), s32[]{:S(2)}) async-start(), calls=%async_computation.4 | async-start | bytes 3244032 | tf_op jit(solution)/shard_map/all_gather | solution.py:56
  157.7 48.0 %all-to-all-start = ((bf16[256,64,32]{0,2,1:T(8,128)(2,1)}), bf16[256,64,32]{0,2,1:T(8,128)(2,1)S(1)}, u32[]{:S(2)}, u32[]{:S(2)}) async-start(bf16[256,64,32]{0,2,1:T(8,128)(2,1)} %bitcast.6), calls=%async_computation | async-start | bytes 2097152 | tf_op jit(solution)/shard_map/all_to_all | solution.py:46
  283.4 15.7 %copy-start.1 = (f32[512,2]{0,1:T(2,128)S(1)}, f32[512,2]{0,1:T(2,128)}, u32[]{:S(2)}) copy-start(f32[512,2]{0,1:T(2,128)} %param.12) | copy-start | bytes 12292
  283.4 16.0 %copy-start.2 = (s32[512]{0:T(512)S(1)}, s32[512]{0:T(512)}, u32[]{:S(2)}) copy-start(s32[512]{0:T(512)} %param.17) | copy-start | bytes 6148
  283.4 107.4 %all-to-all-start.1 = ((f32[256,64,32]{0,2,1:T(8,128)}), f32[256,64,32]{0,2,1:T(8,128)S(1)}, u32[]{:S(2)}, u32[]{:S(2)}) async-start(f32[256,64,32]{0,2,1:T(8,128)} %bitcast.43), calls=%async_computation.1 | async-start | bytes 4194304 | tf_op jit(solution)/shard_map/all_to_all | solution.py:65
  391.3 124.3 %copy-start.3 = (f32[32]{0:T(128)S(1)}, f32[32]{0:T(128)}, u32[]{:S(2)}) copy-start(f32[32]{0:T(128)} %param.16) | copy-start | bytes 388
Sparse Core Ops, SparseCore 0:
  10.3 137.3 all-gather.4
  149.8 43.5 all-gather.6
  195.5 39.2 all-gather.10
  236.8 39.2 all-gather.8
where the time goes:
time: 566 us
  waiting for transfers between devices  334 us (59%)
  blocking collectives  159 us (28%)
  starting transfers between devices  24.5 us (4%)
  local copies, waits for them, and re-layouts  16 us (3%)
  between operations  13.4 us (2%)
  matrix products  12 us (2%)
  other arithmetic  6.35 us (1%)
    all_gather x1, waiting for transfers between devices, shards(): lax.all_gather(context, 'mp', axis=1, tiled=True)  133 us
    psum x1, blocking collectives, shards(): squares = lax.psum(jnp.sum(combined * combined, axis=1), 'mp')  118 us
    all_to_all x1, waiting for transfers between devices, shards(): lax.all_to_all(partial_value, 'mp', split_axis=1, concat_axis=0, tiled=True)  91.4 us
    all_gather x1, waiting for transfers between devices, shards(): lax.all_gather(w_up, 'expert', axis=1, tiled=True)  41.3 us
    all_gather x1, blocking collectives, shards(): everyone = lax.all_gather(normed, 'expert', axis=0, tiled=True)  41 us
    all_gather x1, waiting for transfers between devices, shards(): lax.all_gather(w_gate, 'expert', axis=1, tiled=True)  26.9 us
    all_gather x1, waiting for transfers between devices, shards(): lax.all_gather(w_down, 'expert', axis=1, tiled=True)  26.4 us
    all_to_all x1, starting transfers between devices, shards(): lax.all_to_all(partial_value, 'mp', split_axis=1, concat_axis=0, tiled=True)  15.6 us
  transfers between devices with their start and end apart: 6, of which 6 were waited for; matrix products, arithmetic and copies ran while one was open for 3% of the time, Pallas kernels for 0%

commit v1 on v0

--- a/solution.py
+++ b/solution.py
@@ -6,6 +6,19 @@
 EXPERTS = 8
 CAP = 256
 epsilon = 1e-06
+
+
+def collect(x, axis, dim):
+    ways = lax.axis_size(axis)
+    up = [(d, (d + 1) % ways) for d in range(ways)]
+    down = [(d, (d - 1) % ways) for d in range(ways)]
+    earlier, later = ([x], [x])
+    for _ in range(ways // 2):
+        earlier.append(lax.ppermute(earlier[-1], axis, up))
+    for _ in range((ways - 1) // 2):
+        later.append(lax.ppermute(later[-1], axis, down))
+    line = jnp.concatenate([*earlier[::-1], *later[1:]], axis=dim)
+    return jnp.roll(line, (lax.axis_index(axis) - ways // 2) * x.shape[dim], axis=dim)
 
 
 def slot_targets(routes, capacity, experts):
@@ -51,10 +64,7 @@
         preferred_element_type=jnp.float32,
     )
     up_next = jnp.einsum(
-        "rd,hd->rh",
-        inbox_rows,
-        lax.all_gather(w_up, "expert", axis=1, tiled=True),
-        preferred_element_type=jnp.float32,
+        "rd,hd->rh", inbox_rows, collect(w_up, "expert", 1), preferred_element_type=jnp.float32
     )
     activated = (jax.nn.silu(gate_next) * up_next).astype(jnp.bfloat16)
     partial_value = jnp.dot(

time: 566 us -> 529 us (0.935)
  waiting for transfers between devices: 334 us -> 262 us
  starting transfers between devices: 24.5 us -> 46.2 us
  local copies, waits for them, and re-layouts: 16 us -> 28.9 us
    all_gather x1 -> x0, waiting for transfers between devices: 41.3 us -> none  [shards(): lax.all_gather(w_up, 'expert', axis=1, tiled=True)]
    all_gather x1, waiting for transfers between devices: 26.9 us -> 0.01 us  [shards(): lax.all_gather(w_gate, 'expert', axis=1, tiled=True)]
    ppermute x0 -> x7, starting transfers between devices: none -> 21.6 us  [the longest x4 19.6 us: collect(): earlier.append(lax.ppermute(earlier[-1], axis, up))]
    ppermute x0 -> x7, waiting for transfers between devices: none -> 21.4 us  [the longest x4 21 us: collect(): earlier.append(lax.ppermute(earlier[-1], axis, up))]
    all_gather x1, waiting for transfers between devices: 26.4 us -> 13 us  [shards(): lax.all_gather(w_down, 'expert', axis=1, tiled=True)]
    all_to_all x1, waiting for transfers between devices: 12.3 us -> 0.01 us  [shards(): lax.all_to_all(outgoing, 'mp', split_axis=1, concat_axis=1, tiled=True)]
    unnamed x9 -> x26, local copies, waits for them, and re-layouts: 0.85 us -> 13 us
  transfers between devices with their start and end apart: 6 -> 12, of which waited for: 6 -> 8; matrix products, arithmetic and copies ran while one was open for 3% -> 6% of each run, Pallas kernels for 0% -> 0%
where the time goes in v1:
time: 529 us
  waiting for transfers between devices  262 us (50%)
  blocking collectives  159 us (30%)
  starting transfers between devices  46.2 us (9%)
  local copies, waits for them, and re-layouts  28.9 us (5%)
  between operations  13.4 us (3%)
  matrix products  12.6 us (2%)
  other arithmetic  6.35 us (1%)
    all_gather x1, waiting for transfers between devices, shards(): lax.all_gather(context, 'mp', axis=1, tiled=True)  134 us
    psum x1, blocking collectives, shards(): squares = lax.psum(jnp.sum(combined * combined, axis=1), 'mp')  118 us
    all_to_all x1, waiting for transfers between devices, shards(): lax.all_to_all(partial_value, 'mp', split_axis=1, concat_axis=0, tiled=True)  91.4 us
    all_gather x1, blocking collectives, shards(): everyone = lax.all_gather(normed, 'expert', axis=0, tiled=True)  41 us
    ppermute x4, waiting for transfers between devices, collect(): earlier.append(lax.ppermute(earlier[-1], axis, up))  21 us
    ppermute x4, starting transfers between devices, collect(): earlier.append(lax.ppermute(earlier[-1], axis, up))  19.6 us
    all_to_all x1, starting transfers between devices, shards(): lax.all_to_all(partial_value, 'mp', split_axis=1, concat_axis=0, tiled=True)  15.5 us
    all_gather x1, waiting for transfers between devices, shards(): lax.all_gather(w_down, 'expert', axis=1, tiled=True)  13 us
  transfers between devices with their start and end apart: 12, of which 8 were waited for; matrix products, arithmetic and copies ran while one was open for 6% of the time, Pallas kernels for 0%

profile of v1, /device:TPU:1, one launch (start us, length us, event | category | flops | bytes accessed | tf_op | source)
XLA Modules:
  0.0 528.5 jit_solution(10439522784462776525)
XLA Ops:
  8.7 0.8 copy.42
  10.6 2.3 reduce-window.6
  14.0 133.7 %all-gather.4.cloned.1.call-done = bf16[512,2048]{0,1:T(8,128)(2,1)} async-done(((bf16[512,32]{0,1:T(8,128)(2,1)}), bf16[512,2048]{0,1:T(8,128)(2,1)}) %all-gather.4.cloned.1.call-update) | async-done | bytes 2097168 | tf_op jit(solution)/shard_map/all_gather | solution.py:46
  147.7 2.0 convolution_convert_fusion
  149.9 6.4 %scatter_custom_fusion = bf16[2048,32]{1,0:T(8,128)(2,1)S(1)} fusion(s32[1024]{0:T(1024)S(1)} %bitcast.45, bf16[512,32]{1,0:T(8,128)(2,1)S(1)} %copy.44, s32[1024]{0:T(1024)S(1)} %broadcast_clamp_fusion.1, bf16[]{:T(256)} %constant.22.clone.1), kind=kCustom, calls=%fused_computation.18 | custom fusion | bytes 131074 | tf_op jit(solution)/shard_map/scatter | solution.py:55
  156.5 1.2 broadcast_in_dim.10
  157.7 9.0 %all-to-all-start = ((bf16[256,64,32]{0,2,1:T(8,128)(2,1)}), bf16[256,64,32]{0,2,1:T(8,128)(2,1)}, u32[]{:S(2)}, u32[]{:S(2)}) async-start(bf16[256,64,32]{0,2,1:T(8,128)(2,1)} %bitcast.6), calls=%async_computation | async-start | bytes 2097152 | tf_op jit(solution)/shard_map/all_to_all | solution.py:59
  166.7 12.1 %collective-permute-start = (bf16[704,256]{1,0:T(8,128)(2,1)S(1)}, bf16[704,256]{1,0:T(8,128)(2,1)S(1)}, u32[]{:S(2)}, u32[]{:S(2)}) collective-permute-start(bf16[704,256]{1,0:T(8,128)(2,1)S(1)} %copy-done.1), channel_id=1, source_target_pairs={{0,64},{64,128},{128,192},{192,256},{256,320},{320,384},{384,448},... | collective-permute-start | bytes 1081352 | tf_op jit(solution)/shard_map/ppermute | solution.py:17
  178.9 8.2 %collective-permute-done = bf16[704,256]{1,0:T(8,128)(2,1)S(1)} collective-permute-done((bf16[704,256]{1,0:T(8,128)(2,1)S(1)}, bf16[704,256]{1,0:T(8,128)(2,1)S(1)}, u32[]{:S(2)}, u32[]{:S(2)}) %collective-permute-start) | collective-permute-done | bytes 360480 | tf_op jit(solution)/shard_map/ppermute | solution.py:17
  187.1 2.5 collective-permute-start.1
  189.6 0.9 collective-permute-start.4
  190.5 5.5 %collective-permute-done.1 = bf16[704,256]{1,0:T(8,128)(2,1)S(1)} collective-permute-done((bf16[704,256]{1,0:T(8,128)(2,1)S(1)}, bf16[704,256]{1,0:T(8,128)(2,1)S(1)}, u32[]{:S(2)}, u32[]{:S(2)}) %collective-permute-start.1) | collective-permute-done | bytes 360480 | tf_op jit(solution)/shard_map/ppermute | solution.py:17
  196.0 2.5 collective-permute-start.2
  198.6 4.3 collective-permute-done.2
  202.9 2.5 collective-permute-start.3
  205.8 1.1 collective-permute-start.6
  206.9 2.9 collective-permute-done.3
  209.7 0.8 constant_dynamic-update-slice_fusion.15
  212.1 0.8 constant_dynamic-update-slice_fusion.12
  215.4 0.8 constant_dynamic-update-slice_fusion.8
  219.4 0.8 constant_dynamic-update-slice_fusion.3
  221.0 0.8 constant_dynamic-update-slice_fusion.1
  222.7 3.0 fusion.27
  225.7 13.0 %all-gather.8.cloned.1.call-done = bf16[704,2048]{1,0:T(8,128)(2,1)} async-done(((bf16[704,256]{1,0:T(8,128)(2,1)}), bf16[704,2048]{1,0:T(8,128)(2,1)}) %all-gather.8.cloned.1.call-update) | async-done | bytes 2883600 | tf_op jit(solution)/shard_map/all_gather | solution.py:72
  238.7 7.6 %fusion.9 = f32[256,2048]{0,1:T(8,128)} fusion(bf16[704,2048]{1,0:T(8,128)(2,1)} %all-gather.8.cloned.1.call-done, bf16[256,2048]{0,1:T(8,128)(2,1)} %bitcast.7, bf16[704,4096]{1,0:T(8,128)(2,1)} %constant_dynamic-update-slice_fusion, s32[]{:T(128)S(6)} %select_n.40, f32[256,704]{0,1:T(8,128)S(1)} %fusion.27), kind=kOutput, calls=%fused_computation.10 | convolution fusion | flops 1477476352 | bytes 9633796 | tf_op jit(solution)/shard_map/dot_general | solution.py:70
  246.3 15.5 %all-to-all-start.1 = ((f32[256,64,32]{0,2,1:T(8,128)}), f32[256,64,32]{0,2,1:T(8,128)S(1)}, u32[]{:S(2)}, u32[]{:S(2)}) async-start(f32[256,64,32]{0,2,1:T(8,128)} %bitcast.42), calls=%async_computation.1 | async-start | bytes 4194304 | tf_op jit(solution)/shard_map/all_to_all | solution.py:75
  262.2 91.4 %all-to-all-done.1 = f32[256,64,32]{0,2,1:T(8,128)S(1)} async-done(((f32[256,64,32]{0,2,1:T(8,128)}), f32[256,64,32]{0,2,1:T(8,128)S(1)}, u32[]{:S(2)}, u32[]{:S(2)}) %all-to-all-start.1) | async-done | bytes 2097184 | tf_op jit(solution)/shard_map/all_to_all | solution.py:75
  354.1 2.8 gather_fusion
  356.9 2.8 multiply_reduce_fusion
  359.9 118.5 %psum.7 = f32[512]{0:T(512)S(1)} all-reduce(f32[512]{0:T(512)S(1)} %multiply_reduce_fusion.1), channel_id=1, replica_groups=mesh['expert'=8,'mp'=64] {'mp'}, use_global_device_ids=true, to_apply=%region_7.8 | all-reduce | flops 512 | bytes 4096 | tf_op jit(solution)/shard_map/psum | solution.py:83
  478.5 41.0 %all_gather.15 = bf16[4096,32]{0,1:T(8,128)(2,1)S(1)} all-gather(bf16[512,32]{0,1:T(8,128)(2,1)S(1)} %multiply_convert_fusion), channel_id=1, replica_groups=mesh['expert'=8,'mp'=64] {'expert'}, dimensions={0}, use_global_device_ids=true | all-gather | bytes 294912 | tf_op jit(solution)/shard_map/all_gather | solution.py:87
  519.9 1.3 gather_fusion.1
  (64 shorter events, 16.1 us)
Async XLA Ops:
  6.5 141.2 %copy-start = (bf16[32,2048]{1,0:T(8,128)(2,1)S(1)}, bf16[32,2048]{1,0:T(8,128)(2,1)}, u32[]{:S(2)}) copy-start(bf16[32,2048]{1,0:T(8,128)(2,1)} %param.10) | copy-start | bytes 393220
  6.5 160.2 %copy-start.1 = (bf16[704,256]{1,0:T(8,128)(2,1)S(1)}, bf16[704,256]{1,0:T(8,128)(2,1)}, u32[]{:S(2)}) copy-start(bf16[704,256]{1,0:T(8,128)(2,1)} %param.14) | copy-start | bytes 1081348
  6.5 141.2 %all-gather.4.cloned.1.call-start = ((), (), s32[]{:S(2)}) async-start(), calls=%async_computation.2 | async-start | bytes 2129920 | tf_op jit(solution)/shard_map/all_gather | solution.py:46
  7.3 215.4 %all-gather.6.cloned.1.call-start = ((), (), s32[]{:S(2)}) async-start(), calls=%async_computation.3 | async-start | bytes 3244032 | tf_op jit(solution)/shard_map/all_gather | solution.py:63
  8.0 230.7 %all-gather.8.cloned.1.call-start = ((), (), s32[]{:S(2)}) async-start(), calls=%async_computation.4 | async-start | bytes 3244032 | tf_op jit(solution)/shard_map/all_gather | solution.py:72
  157.7 65.0 %all-to-all-start = ((bf16[256,64,32]{0,2,1:T(8,128)(2,1)}), bf16[256,64,32]{0,2,1:T(8,128)(2,1)}, u32[]{:S(2)}, u32[]{:S(2)}) async-start(bf16[256,64,32]{0,2,1:T(8,128)(2,1)} %bitcast.6), calls=%async_computation | async-start | bytes 2097152 | tf_op jit(solution)/shard_map/all_to_all | solution.py:59
  166.7 20.4 %collective-permute-start = (bf16[704,256]{1,0:T(8,128)(2,1)S(1)}, bf16[704,256]{1,0:T(8,128)(2,1)S(1)}, u32[]{:S(2)}, u32[]{:S(2)}) collective-permute-start(bf16[704,256]{1,0:T(8,128)(2,1)S(1)} %copy-done.1), channel_id=1, source_target_pairs={{0,64},{64,128},{128,192},{192,256},{256,320},{320,384},{384,448},... | collective-permute-start | bytes 1081352 | tf_op jit(solution)/shard_map/ppermute | solution.py:17
  187.1 8.9 %collective-permute-start.1 = (bf16[704,256]{1,0:T(8,128)(2,1)S(1)}, bf16[704,256]{1,0:T(8,128)(2,1)S(1)}, u32[]{:S(2)}, u32[]{:S(2)}) collective-permute-start(bf16[704,256]{1,0:T(8,128)(2,1)S(1)} %collective-permute-done), channel_id=1, source_target_pairs={{0,64},{64,128},{128,192},{192,256},{256,320},{320,384},{384,448},... | collective-permute-start | bytes 1081352 | tf_op jit(solution)/shard_map/ppermute | solution.py:17
  189.6 8.9 %collective-permute-start.4 = (bf16[704,256]{1,0:T(8,128)(2,1)S(1)}, bf16[704,256]{1,0:T(8,128)(2,1)S(1)}, u32[]{:S(2)}, u32[]{:S(2)}) collective-permute-start(bf16[704,256]{1,0:T(8,128)(2,1)S(1)} %copy-done.1), channel_id=1, source_target_pairs={{0,448},{64,0},{128,64},{192,128},{256,192},{320,256},{384,320},{4... | collective-permute-start | bytes 1081352 | tf_op jit(solution)/shard_map/ppermute | solution.py:19
  196.0 6.9 %collective-permute-start.2 = (bf16[704,256]{1,0:T(8,128)(2,1)S(1)}, bf16[704,256]{1,0:T(8,128)(2,1)S(1)}, u32[]{:S(2)}, u32[]{:S(2)}) collective-permute-start(bf16[704,256]{1,0:T(8,128)(2,1)S(1)} %collective-permute-done.1), channel_id=1, source_target_pairs={{0,64},{64,128},{128,192},{192,256},{256,320},{320,384},{384,448},... | collective-permute-start | bytes 1081352 | tf_op jit(solution)/shard_map/ppermute | solution.py:17
  198.5 7.3 %collective-permute-start.5 = (bf16[704,256]{1,0:T(8,128)(2,1)S(1)}, bf16[704,256]{1,0:T(8,128)(2,1)S(1)}, u32[]{:S(2)}, u32[]{:S(2)}) collective-permute-start(bf16[704,256]{1,0:T(8,128)(2,1)S(1)} %collective-permute-done.4), channel_id=1, source_target_pairs={{0,448},{64,0},{128,64},{192,128},{256,192},{320,256},{384,320},{4... | collective-permute-start | bytes 1081352 | tf_op jit(solution)/shard_map/ppermute | solution.py:19
  202.9 6.9 %collective-permute-start.3 = (bf16[704,256]{1,0:T(8,128)(2,1)S(1)}, bf16[704,256]{1,0:T(8,128)(2,1)S(1)}, u32[]{:S(2)}, u32[]{:S(2)}) collective-permute-start(bf16[704,256]{1,0:T(8,128)(2,1)S(1)} %collective-permute-done.2), channel_id=1, source_target_pairs={{0,64},{64,128},{128,192},{192,256},{256,320},{320,384},{384,448},... | collective-permute-start | bytes 1081352 | tf_op jit(solution)/shard_map/ppermute | solution.py:17
  205.8 9.6 %collective-permute-start.6 = (bf16[704,256]{1,0:T(8,128)(2,1)S(1)}, bf16[704,256]{1,0:T(8,128)(2,1)S(1)}, u32[]{:S(2)}, u32[]{:S(2)}) collective-permute-start(bf16[704,256]{1,0:T(8,128)(2,1)S(1)} %collective-permute-done.5), channel_id=1, source_target_pairs={{0,448},{64,0},{128,64},{192,128},{256,192},{320,256},{384,320},{4... | collective-permute-start | bytes 1081352 | tf_op jit(solution)/shard_map/ppermute | solution.py:19
  225.7 36.2 %copy-start.2 = (f32[512,2]{0,1:T(2,128)S(1)}, f32[512,2]{0,1:T(2,128)}, u32[]{:S(2)}) copy-start(f32[512,2]{0,1:T(2,128)} %param.12) | copy-start | bytes 12292
  225.7 36.5 %copy-start.3 = (s32[512]{0:T(512)S(1)}, s32[512]{0:T(512)}, u32[]{:S(2)}) copy-start(s32[512]{0:T(512)} %param.17) | copy-start | bytes 6148
  246.3 107.3 %all-to-all-start.1 = ((f32[256,64,32]{0,2,1:T(8,128)}), f32[256,64,32]{0,2,1:T(8,128)S(1)}, u32[]{:S(2)}, u32[]{:S(2)}) async-start(f32[256,64,32]{0,2,1:T(8,128)} %bitcast.42), calls=%async_computation.1 | async-start | bytes 4194304 | tf_op jit(solution)/shard_map/all_to_all | solution.py:75
  261.9 216.5 %copy-start.4 = (f32[32]{0:T(128)S(1)}, f32[32]{0:T(128)}, u32[]{:S(2)}) copy-start(f32[32]{0:T(128)} %param.16) | copy-start | bytes 388
Sparse Core Ops, SparseCore 0:
  10.3 137.3 all-gather.3
  149.8 46.8 all-gather.5
  198.8 39.8 all-gather.7
